TPU v7x, 32 devices: a whole 2x2x4 slice. The times are simulated.
32 devices in a mesh: snode: 16 (over z, y, x), row: 2 (over core).
Axes of the slice: x: 2, y: 2, z: 4, core: 2. Of those that a mesh axis runs over, the one named last changes fastest.
Arguments:
- ancestor_sigma: bfloat16 [8192, 8192], P('row', 'snode'), may hold values from -8 to 8, as said below
- child_panels: bfloat16 [96, 4096, 128], P('snode', 'row'), may hold values from -1 to 1
- diagonal_inverse_blocks: float32 [96, 128, 128], P('snode', 'row'), may hold values from -4 to 4, as said below
- block_list: int32 [96, 32], P('snode'), may hold values from 0 to 63, as said below
- block_count: int32 [96], P('snode'), may hold values from 8 to 32, as said below
- child_width: int32 [96], P('snode'), may hold values from 64 to 128, as said below
- owner_slot: int32 [64], replicated, may hold values from 0 to 63, each once
Outputs:
- selected_panel_inverse: float32 [8192, 96, 128], P('row', 'snode')
- selected_diagonal_inverse: float32 [96, 128, 128], P('snode', 'row')
Inputs may be any that keep to these rules, and one draw needn't show every extreme that they name: `ancestor_sigma`: symmetric. `diagonal_inverse_blocks`: each child's block is symmetric. `block_list`: the 32 entries of a row are distinct and ascending. `block_count`: some child has exactly 32. `child_width`: some child has exactly 128.
All inputs are finite; a program needn't handle non-finite values.
Results may differ from a plain program's by a relative error of at most 0.0003.
Values may be sent and summed in bfloat16 or wider, within the bound.
No kernel may reach another device: no remote copies, remote signals or barrier semaphores. Data moves between devices by JAX's collectives and lax.ppermute only.
A program may use at most 192 MiB of HBM per device.

v0:
```python
import jax
import jax.numpy as jnp
from jax import lax
from jax.sharding import PartitionSpec as P

B = 128
KMAX = 32
WJ = 128
NB = 64


def slot_table(block_list, block_count, child_width, owner_slot):
    block_ids = jnp.arange(NB, dtype=jnp.int32)
    named = block_list[:, :, None] == block_ids[None, None, :]
    slot_ids = jnp.sum(jnp.where(named, owner_slot[None, None, :], 0), axis=2)
    valid_blocks = jnp.arange(KMAX, dtype=jnp.int32)[None, :] < block_count[:, None]
    placed = (slot_ids[:, :, None] == block_ids[None, None, :]) & valid_blocks[:, :, None]
    active_columns = jnp.arange(WJ, dtype=jnp.int32)[None, :] < child_width[:, None]
    return (placed, active_columns)


def expand_rows(place_table, blocks):
    children = blocks.shape[0]
    spread = jnp.einsum("ckn,ckbj->nbcj", place_table, blocks, preferred_element_type=jnp.float32)
    return spread.astype(jnp.bfloat16).reshape(place_table.shape[2] * B, children * WJ)


def body(
    ancestor_sigma,
    child_panels,
    diagonal_inverse_blocks,
    block_list,
    block_count,
    child_width,
    owner_slot,
):
    row_devices = lax.axis_size("row")
    row_positions = lax.axis_index("row")
    children = child_panels.shape[0]
    local_rows = ancestor_sigma.shape[0]
    placed, active_columns = slot_table(block_list, block_count, child_width, owner_slot)
    place_bf = placed.astype(jnp.bfloat16)
    if row_devices == 2:
        partner = lax.ppermute(child_panels, "row", [(0, 1), (1, 0)])
        first = row_positions == 0
        gathered = jnp.concatenate(
            [jnp.where(first, child_panels, partner), jnp.where(first, partner, child_panels)],
            axis=1,
        )
    else:
        gathered = lax.all_gather(child_panels, "row", axis=1, tiled=True)
    blocks = gathered.reshape(children, KMAX, B, WJ)
    blocks = jnp.where(active_columns[:, None, None, :], blocks, jnp.zeros_like(blocks))
    panel_rows = expand_rows(place_bf, blocks)
    flipped = lax.all_gather(ancestor_sigma.T, "snode", axis=0, tiled=True)
    product = lax.dot_general(
        flipped, panel_rows, (((0,), (0,)), ((), ())), preferred_element_type=jnp.float32
    )
    product_table = product.reshape(local_rows, children, WJ)
    own_blocks = local_rows // B
    own_table = lax.dynamic_slice_in_dim(place_bf, row_positions * own_blocks, own_blocks, 2)
    own_rows = expand_rows(own_table, blocks).reshape(local_rows, children, WJ)
    partial_value = jnp.einsum(
        "nca,ncb->cab", own_rows.astype(jnp.float32), product_table, precision=lax.Precision.HIGHEST
    )
    shared_rows = WJ // row_devices
    if row_devices == 2:
        reduced_total = partial_value + lax.ppermute(partial_value, "row", [(0, 1), (1, 0)])
    else:
        reduced_total = lax.psum(partial_value, "row")
    reduced_total = lax.dynamic_slice_in_dim(
        reduced_total, row_positions * shared_rows, shared_rows, 1
    )
    active_flags = active_columns.astype(jnp.float32)
    owned_active = lax.dynamic_slice_in_dim(
        active_flags, row_positions * shared_rows, shared_rows, 1
    )
    selected_diagonal_inverse = (
        (diagonal_inverse_blocks + reduced_total)
        * owned_active[:, :, None]
        * active_flags[:, None, :]
    )
    slot_live = jnp.sum(placed.astype(jnp.float32), axis=1)
    own_slots = lax.dynamic_slice_in_dim(slot_live, row_positions * own_blocks, own_blocks, 1)
    active_rows = jnp.repeat(own_slots.T, B, axis=0)
    selected_panel_inverse = -product_table * active_rows[:, :, None] * active_flags[None, :, :]
    return (selected_panel_inverse, selected_diagonal_inverse)


def solution(mesh):
    placed = (
        P("row", "snode"),
        P("snode", "row", None),
        P("snode", "row", None),
        P("snode", None),
        P("snode"),
        P("snode"),
        P(),
    )
    return jax.shard_map(
        body,
        mesh=mesh,
        in_specs=placed,
        out_specs=(P("row", "snode", None), P("snode", "row", None)),
        check_vma=False,
    )
```

profile of v0, /device:TPU:1, one launch (start us, length us, event | category | flops | bytes accessed | tf_op | source)
XLA Modules:
  0.0 898.8 jit_solution(4280391396216717396)
XLA Ops:
  7.2 0.7 all-gather.2.cloned.1.call-update
  7.9 0.1 collective-permute-start
  8.0 1.0 select_reduce_fusion
  9.1 0.7 iota_compare_fusion.2
  9.8 0.1 convert_reduce_fusion
  9.9 0.1 dynamic-slice_bitcast_fusion
  10.0 0.1 broadcast_bitcast_fusion
  10.1 0.1 copy.45
  10.2 0.7 fusion.16
  10.9 0.1 constant_dynamic-slice_fusion
  11.0 3.0 collective-permute-done
  14.0 2.3 broadcast_select_fusion.1
  16.3 0.4 pad_maximum_fusion
  16.7 4.0 convert_bitcast_fusion.1
  20.7 5.8 copy.24
  26.4 7.1 convert_bitcast_fusion
  33.5 18.0 %copy.22 = bf16[64,128,6,128]{1,0,3,2:T(8,128)(2,1)} copy(bf16[64,128,6,128]{3,0,1,2:T(8,128)(2,1)} %convert_bitcast_fusion) | data formatting | bytes 25165824 | tf_op jit(solution)/shard_map/convert_element_type | solution.py:25
  51.4 685.6 %all-gather.2.cloned.1.call-done = bf16[8192,4096]{0,1:T(8,128)(2,1)} async-done(((bf16[512,4096]{0,1:T(8,128)(2,1)}), bf16[8192,4096]{0,1:T(8,128)(2,1)}) %all-gather.2.cloned.1.call-update) | async-done | bytes 67108880 | tf_op jit(solution)/shard_map/all_gather | solution.py:55
  737.1 117.5 %fusion = f32[768,4096]{1,0:T(8,128)} fusion(bf16[8192,4096]{0,1:T(8,128)(2,1)} %all-gather.2.cloned.1.call-done, bf16[96,8,64,128]{3,2,1,0:T(8,128)(2,1)} %bitcast.44), kind=kOutput, calls=%fused_computation | convolution fusion | flops 51539607552 | bytes 92274688 | tf_op jit(solution)/shard_map/dot_general | solution.py:56
  854.6 12.6 %copy.23 = f32[4096,6,128]{2,0,1:T(8,128)} copy(f32[4096,6,128]{0,2,1:T(8,128)} %bitcast.39) | data formatting | bytes 25165824 | tf_op jit(solution)/shard_map/reshape | solution.py:59
  867.2 11.1 %fusion.18 = f32[6,128,128]{2,1,0:T(8,128)S(1)} fusion(bf16[4096,6,128]{2,0,1:T(8,128)(2,1)} %bitcast.43, f32[4096,6,128]{0,2,1:T(8,128)} %bitcast.40), kind=kOutput, calls=%fused_computation.35 | convolution fusion | flops 4831838208 | bytes 19267584 | tf_op jit(solution)/shard_map/nca,ncb->cab/dot_general | solution.py:63
  878.3 1.2 collective-permute-start.1
  879.4 11.7 %multiply_multiply_fusion = f32[4096,6,128]{2,0,1:T(8,128)} fusion(f32[4096,6,128]{2,0,1:T(8,128)} %copy.23, f32[6,128]{1,0:T(8,128)S(1)} %get-tuple-element.4, f32[4096,6]{0,1:T(8,128)S(1)} %bitcast.46), kind=kLoop, calls=%fused_computation.3 | loop fusion | flops 9437184 | bytes 25267200 | tf_op jit(solution)/shard_map/mul | solution.py:86
  891.1 0.8 fusion.8
  (7 shorter events, 0.1 us)
Async XLA Ops:
  7.2 6.8 copy-start
  7.2 729.9 %all-gather.2.cloned.1.call-start = ((), (), s32[]{:S(2)}) async-start(), calls=%async_computation | async-start | bytes 71303168 | tf_op jit(solution)/shard_map/all_gather | solution.py:55
  7.9 6.1 collective-permute-start
  878.3 12.8 %collective-permute-start.1 = (f32[6,128,128]{2,1,0:T(8,128)S(1)}, f32[6,128,128]{2,1,0:T(8,128)S(1)}, u32[]{:S(2)}, u32[]{:S(2)}) collective-permute-start(f32[6,128,128]{2,1,0:T(8,128)S(1)} %fusion.18), channel_id=1, source_target_pairs={{0,1},{1,0},{2,3},{3,2},{4,5},{5,4},{6,7},{7,6},{8,9},{9,8},{10,11... | collective-permute-start | bytes 1179656 | tf_op jit(solution)/shard_map/ppermute | solution.py:68
  879.4 11.7 %copy-start.1 = (f32[6,64,128]{2,1,0:T(8,128)S(1)}, f32[6,64,128]{2,1,0:T(8,128)}, u32[]{:S(2)}) copy-start(f32[6,64,128]{2,1,0:T(8,128)} %param.9) | copy-start | bytes 589828
Sparse Core Ops, SparseCore 0:
  10.8 726.2 all-gather.1
where the time goes:
time: 900 us; the launch traced here: 899 us
  waiting for transfers between devices  689 us (77%)
  matrix products  140 us (16%)
  local copies, waits for them, and re-layouts  36.6 us (4%)
  other arithmetic  17.9 us (2%)
  between operations  14.1 us (2%)
    all_gather x1, waiting for transfers between devices, body(): flipped = lax.all_gather(ancestor_sigma.T, 'snode', axis=0, tiled=True)  686 us
    dot_general x1, matrix products, body(): lax.dot_general(flipped, panel_rows, (((0,), (0,)), ((), ())), preferred_...  118 us
    convert_element_type x2, local copies, waits for them, and re-layouts, expand_rows(): spread.astype(jnp.bfloat16).reshape(place_table.shape[2] * B, children * WJ)  23.7 us
  transfers between devices with their start and end apart: 3, of which 2 were waited for; matrix products, arithmetic and copies ran while one was open for 6% of the time, Pallas kernels for 0%

commit v1 on v0

--- a/solution.py
+++ b/solution.py
@@ -52,7 +52,15 @@
     blocks = gathered.reshape(children, KMAX, B, WJ)
     blocks = jnp.where(active_columns[:, None, None, :], blocks, jnp.zeros_like(blocks))
     panel_rows = expand_rows(place_bf, blocks)
-    flipped = lax.all_gather(ancestor_sigma.T, "snode", axis=0, tiled=True)
+    ways, here = (lax.axis_size("snode"), lax.axis_index("snode"))
+    grown, reach = (ancestor_sigma.T, 1)
+    while reach < ways:
+        theirs = lax.ppermute(grown, "snode", [(d, d ^ reach) for d in range(ways)])
+        mine_first = jnp.concatenate([grown, theirs], axis=0)
+        theirs_first = jnp.concatenate([theirs, grown], axis=0)
+        grown = jnp.where(here & reach == 0, mine_first, theirs_first)
+        reach = 2 * reach
+    flipped = grown
     product = lax.dot_general(
         flipped, panel_rows, (((0,), (0,)), ((), ())), preferred_element_type=jnp.float32
     )

time: 900 us -> 2270 us (2.52)
  waiting for transfers between devices: 689 us -> 2010 us
  other arithmetic: 17.9 us -> 70.5 us
    ppermute x0 -> x4, waiting for transfers between devices: none -> 2010 us  [body(): theirs = lax.ppermute(grown, 'snode', [(d, d ^ reach) for d in range(ways)])]
    all_gather x1 -> x0, waiting for transfers between devices: 686 us -> none  [body(): flipped = lax.all_gather(ancestor_sigma.T, 'snode', axis=0, tiled=True)]
    select_n x0 -> x3, other arithmetic: none -> 66.4 us  [body(): grown = jnp.where(here & reach == 0, mine_first, theirs_first)]
  transfers between devices with their start and end apart: 3 -> 6, of which waited for: 2 -> 6; matrix products, arithmetic and copies ran while one was open for 6% -> 2% of each run, Pallas kernels for 0% -> 0%
where the time goes in v1:
time: 2270 us
  waiting for transfers between devices  2010 us (89%)
  matrix products  138 us (6%)
  other arithmetic  70.5 us (3%)
  local copies, waits for them, and re-layouts  39.2 us (2%)
    ppermute x4, waiting for transfers between devices, body(): theirs = lax.ppermute(grown, 'snode', [(d, d ^ reach) for d in range(ways)])  2010 us
    dot_general x1, matrix products, body(): lax.dot_general(flipped, panel_rows, (((0,), (0,)), ((), ())), preferred_...  115 us
    select_n x3, other arithmetic, body(): grown = jnp.where(here & reach == 0, mine_first, theirs_first)  66.4 us
  transfers between devices with their start and end apart: 6, of which 6 were waited for; matrix products, arithmetic and copies ran while one was open for 2% of the time, Pallas kernels for 0%

profile of v1, /device:TPU:1, one launch (start us, length us, event | category | flops | bytes accessed | tf_op | source)
XLA Modules:
  0.0 2272.0 jit_solution(3923170294093734676)
XLA Ops:
  0.6 2.1 collective-permute-start
  2.7 90.6 %collective-permute-done = bf16[512,4096]{0,1:T(8,128)(2,1)} collective-permute-done((bf16[512,4096]{0,1:T(8,128)(2,1)}, bf16[512,4096]{0,1:T(8,128)(2,1)}, u32[]{:S(2)}, u32[]{:S(2)}) %collective-permute-start) | collective-permute-done | bytes 4194336 | tf_op jit(solution)/shard_map/ppermute | solution.py:58
  93.3 11.5 maximum_select_fusion.3
  104.9 1.2 collective-permute-start.1
  106.0 179.9 %collective-permute-done.1 = bf16[1024,4096]{0,1:T(8,128)(2,1)} collective-permute-done((bf16[1024,4096]{0,1:T(8,128)(2,1)}, bf16[1024,4096]{0,1:T(8,128)(2,1)}, u32[]{:S(2)}, u32[]{:S(2)}) %collective-permute-start.1) | collective-permute-done | bytes 8388640 | tf_op jit(solution)/shard_map/ppermute | solution.py:58
  285.9 20.7 maximum_select_fusion.2
  306.6 0.9 collective-permute-start.2
  307.5 358.9 %collective-permute-done.2 = bf16[2048,4096]{0,1:T(8,128)(2,1)} collective-permute-done((bf16[2048,4096]{0,1:T(8,128)(2,1)}, bf16[2048,4096]{0,1:T(8,128)(2,1)}, u32[]{:S(2)}, u32[]{:S(2)}) %collective-permute-start.2) | collective-permute-done | bytes 16777248 | tf_op jit(solution)/shard_map/ppermute | solution.py:58
  666.5 34.2 %maximum_select_fusion.1 = bf16[4096,4096]{0,1:T(8,128)(2,1)} fusion(bf16[2048,4096]{0,1:T(8,128)(2,1)} %collective-permute-done.2, bf16[2048,4096]{0,1:T(8,128)(2,1)} %maximum_select_fusion.2, pred[]{:T(512)S(6)} %eq.42), kind=kLoop, calls=%fused_computation.4 | loop fusion | flops 150994944 | bytes 67108864 | tf_op jit(solution)/shard_map/jit(_where)/select_n | solution.py:61
  700.7 1.7 collective-permute-start.3
  702.3 3.7 collective-permute-start.4
  706.8 4.6 collective-permute-done.4
  711.4 2.3 broadcast_select_fusion.1
  714.1 4.0 convert_bitcast_fusion.1
  718.1 5.2 copy.19
  723.3 7.1 convert_bitcast_fusion
  730.3 17.9 copy.18
  748.2 15.8 copy.35
  764.0 1378.3 %collective-permute-done.3 = bf16[4096,4096]{0,1:T(8,128)(2,1)} collective-permute-done((bf16[4096,4096]{0,1:T(8,128)(2,1)}, bf16[4096,4096]{0,1:T(8,128)(2,1)}, u32[]{:S(2)}, u32[]{:S(2)}) %collective-permute-start.3) | collective-permute-done | bytes 33554464 | tf_op jit(solution)/shard_map/ppermute | solution.py:58
  2142.3 115.3 %multiply_multiply_fusion = (f32[4096,6,128]{2,0,1:T(8,128)}, f32[4096,6,128]{2,0,1:T(8,128)}) fusion(f32[6,128]{1,0:T(8,128)S(1)} %get-tuple-element.4, f32[4096,6]{0,1:T(8,128)S(1)} %bitcast.54, bf16[6,128,8192]{2,1,0:T(8,128)(2,1)} %bitcast.51, bf16[4096,4096]{0,1:T(8,128)(2,1)} %collective-permute-done.3, bf16[4096,4096]{0,1:T(8,128)(2,1)} %maximum_select_fusion.1, ...), kind=kOutput, calls=%fused_computation.7 | convolution fusion | flops 51851034624 | bytes 104958976 | tf_op jit(solution)/shard_map/dot_general | solution.py:64
  2257.6 11.3 fusion.20
  2268.9 0.9 collective-permute-start.5
  2269.9 1.3 collective-permute-done.5
  2271.2 0.8 fusion.9
  (22 shorter events, 1.3 us)
Async XLA Ops:
  0.6 92.7 %collective-permute-start = (bf16[512,4096]{0,1:T(8,128)(2,1)}, bf16[512,4096]{0,1:T(8,128)(2,1)}, u32[]{:S(2)}, u32[]{:S(2)}) collective-permute-start(bf16[512,4096]{0,1:T(8,128)(2,1)} %bitcast.52), channel_id=1, source_target_pairs={{0,2},{2,0},{4,6},{6,4},{8,10},{10,8},{12,14},{14,12},{16,18},{18,... | collective-permute-start | bytes 12582920 | tf_op jit(solution)/shard_map/ppermute | solution.py:58
  104.9 181.0 %collective-permute-start.1 = (bf16[1024,4096]{0,1:T(8,128)(2,1)}, bf16[1024,4096]{0,1:T(8,128)(2,1)}, u32[]{:S(2)}, u32[]{:S(2)}) collective-permute-start(bf16[1024,4096]{0,1:T(8,128)(2,1)} %maximum_select_fusion.3), channel_id=1, source_target_pairs={{0,4},{2,6},{4,0},{6,2},{8,12},{10,14},{12,8},{14,10},{16,20},{18,... | collective-permute-start | bytes 25165832 | tf_op jit(solution)/shard_map/ppermute | solution.py:58
  306.6 359.9 %collective-permute-start.2 = (bf16[2048,4096]{0,1:T(8,128)(2,1)}, bf16[2048,4096]{0,1:T(8,128)(2,1)}, u32[]{:S(2)}, u32[]{:S(2)}) collective-permute-start(bf16[2048,4096]{0,1:T(8,128)(2,1)} %maximum_select_fusion.2), channel_id=1, source_target_pairs={{0,8},{2,10},{4,12},{6,14},{8,0},{10,2},{12,4},{14,6},{16,24},{18,... | collective-permute-start | bytes 50331656 | tf_op jit(solution)/shard_map/ppermute | solution.py:58
  307.5 394.8 %copy-start = (bf16[6,2048,128]{2,1,0:T(8,128)(2,1)S(1)}, bf16[6,2048,128]{2,1,0:T(8,128)(2,1)}, u32[]{:S(2)}) copy-start(bf16[6,2048,128]{2,1,0:T(8,128)(2,1)} %param.8) | copy-start | bytes 9437188
  307.5 398.5 %copy-start.2 = (s32[6,32]{1,0:T(8,128)S(1)}, s32[6,32]{1,0:T(8,128)}, u32[]{:S(2)}) copy-start(s32[6,32]{1,0:T(8,128)} %param.10) | copy-start | bytes 2308
  307.5 398.5 %copy-start.3 = (s32[64]{0:T(128)S(1)}, s32[64]{0:T(128)}, u32[]{:S(2)}) copy-start(s32[64]{0:T(128)} %param.13) | copy-start | bytes 772
  307.5 398.8 %copy-start.5 = (s32[6]{0:T(128)S(1)}, s32[6]{0:T(128)}, u32[]{:S(2)}) copy-start(s32[6]{0:T(128)} %param.11) | copy-start | bytes 76
  307.5 399.2 %copy-start.4 = (s32[6]{0:T(128)S(1)}, s32[6]{0:T(128)}, u32[]{:S(2)}) copy-start(s32[6]{0:T(128)} %param.12) | copy-start | bytes 76
  700.7 1441.6 %collective-permute-start.3 = (bf16[4096,4096]{0,1:T(8,128)(2,1)}, bf16[4096,4096]{0,1:T(8,128)(2,1)}, u32[]{:S(2)}, u32[]{:S(2)}) collective-permute-start(bf16[4096,4096]{0,1:T(8,128)(2,1)} %maximum_select_fusion.1), channel_id=1, source_target_pairs={{0,16},{2,18},{4,20},{6,22},{8,24},{10,26},{12,28},{14,30},{16,0},... | collective-permute-start | bytes 100663304 | tf_op jit(solution)/shard_map/ppermute | solution.py:58
  702.3 9.1 collective-permute-start.4
  2257.6 13.6 copy-start.1
  2268.9 2.3 collective-permute-start.5
